TPU v7x, 256 devices: a whole 4x4x8 slice. The times are simulated.
256 devices in a mesh: tm: 2 (over core), scen: 4 (over x), line: 32 (over z, y).
Axes of the slice: x: 4, y: 4, z: 8, core: 2. Of those that a mesh axis runs over, the one named last changes fastest.
Arguments:
- line_blocks: bfloat16 [64, 128, 1024], P('line'), may hold values from -0.1875 to 0.1875
- binding: int32 [128, 2, 8], P(('scen', 'line'), 'tm'), may hold values from 0 to 63, as said below
- line_weight: float32 [128, 2, 8, 128], P(('scen', 'line'), 'tm'), may hold values from 0.25 to 4
- barrier: float32 [128, 2, 1024], P(('scen', 'line'), 'tm'), may hold values from 0.5 to 4
- gradient: float32 [128, 2, 1024], P(('scen', 'line'), 'tm'), may hold values from -6 to 6
- link_columns: bfloat16 [128, 2, 1024, 128], P(('scen', 'line'), 'tm'), may hold values from -0.5 to 0.5
- ramp_weight: float32 [256], replicated, may hold values from 10 to 200
- link_diag: float32 [128], replicated, may hold values from 0.5 to 5
- link_rhs: float32 [128], replicated, may hold values from -18 to 18
Outputs:
- newton_step: float32 [128, 2, 1024], P(('scen', 'line'), 'tm')
- link_step: float32 [128], replicated
Inputs may be any that keep to these rules, and one draw needn't show every extreme that they name: Block numbers b are held by line device b // 2. Take the list binding[s, t] of one scenario s and period t: exactly one line device holds 2 of its blocks, no line device holds more, and the other blocks are spread as evenly as possible over the other line devices, in a shuffled order. A block may appear more than once.
All inputs are finite; a program needn't handle non-finite values.
Results may differ from a plain program's by a relative error of at most 0.00084.
Values may be sent and summed in bfloat16 or wider, within the bound.
No kernel may reach another device: no remote copies, remote signals or barrier semaphores. Data moves between devices by JAX's collectives and lax.ppermute only.
A program may use at most 128 MiB of HBM per device.

v0:
```python
import jax
import jax.numpy as jnp
from jax import lax
from jax.sharding import PartitionSpec as P

highest = lax.Precision.HIGHEST


def period_hessian(selected, weights, barrier_row, ramp_weight, end_factor):
    order = selected.shape[-1]
    scaled = (weights[:, :, None] * selected.astype(jnp.float32)).astype(jnp.bfloat16)
    flat = selected.reshape(-1, order)
    scaled_flat = scaled.reshape(-1, order)
    hessian = lax.dot_general(
        flat, scaled_flat, (((0,), (0,)), ((), ())), preferred_element_type=jnp.float32
    )
    count = ramp_weight.shape[0]
    extra = jnp.concatenate([end_factor * ramp_weight, jnp.zeros((order - count,), jnp.float32)])
    return hessian + jnp.diag(barrier_row + extra)


def butterfly_sum(value, axes):
    for axis in axes:
        size = lax.axis_size(axis)
        step = 1
        while step < size:
            pairs = [(i, i ^ step) for i in range(size)]
            value = value + lax.ppermute(value, axis, pairs)
            step *= 2
    return value


def trsm(a, b, transpose=False):
    return lax.linalg.triangular_solve(a, b, left_side=True, lower=True, transpose_a=transpose)


def on_device(
    line_blocks,
    binding,
    line_weight,
    barrier,
    gradient,
    link_columns,
    ramp_weight,
    link_diag,
    link_rhs,
):
    block_ids = binding[0, 0]
    order = line_blocks.shape[2]
    count = ramp_weight.shape[0]
    links = link_columns.shape[-1]
    every_block = lax.all_gather(line_blocks, "line", axis=0, tiled=True)
    selected = jnp.take(every_block, block_ids, axis=0)
    shard = lax.axis_index("tm")
    shards = lax.axis_size("tm")
    end_factor = jnp.where((shard == 0) | (shard == shards - 1), 1.0, 2.0).astype(jnp.float32)
    hessian = period_hessian(selected, line_weight[0, 0], barrier[0, 0], ramp_weight, end_factor)
    link_float = link_columns[0, 0].astype(jnp.float32)
    rhs = jnp.concatenate([gradient[0, 0][:, None], link_float], axis=1)
    h_nn = hessian[count:, count:]
    h_nr = hessian[count:, :count]
    h_rr = hessian[:count, :count]
    l_nn = lax.linalg.cholesky(h_nn)
    solved = trsm(l_nn, jnp.concatenate([h_nr, rhs[count:]], axis=1))
    x_nr = solved[:, :count]
    y_n = solved[:, count:]
    schur = h_rr - jnp.dot(x_nr.T, x_nr, precision=highest)
    reduced = rhs[:count] - jnp.dot(x_nr.T, y_n, precision=highest)
    mine = jnp.concatenate([schur, reduced], axis=1)
    other = lax.ppermute(mine, "tm", [(0, 1), (1, 0)])
    first = shard == 0
    part0 = jnp.where(first, mine, other)
    part1 = jnp.where(first, other, mine)
    coupling = -jnp.diag(ramp_weight)
    system = jnp.concatenate(
        [
            jnp.concatenate([part0[:, :count], coupling], axis=1),
            jnp.concatenate([coupling, part1[:, :count]], axis=1),
        ],
        axis=0,
    )
    lower = lax.linalg.cholesky(system)
    ramp_both = jax.scipy.linalg.cho_solve(
        (lower, True), jnp.concatenate([part0[:, count:], part1[:, count:]], axis=0)
    )
    x_r = jnp.where(first, ramp_both[:count], ramp_both[count:])
    x_n = trsm(l_nn, y_n - jnp.dot(x_nr, x_r, precision=highest), transpose=True)
    solution_cols = jnp.concatenate([x_r, x_n], axis=0)
    step_vec = solution_cols[:, 0]
    step_cols = solution_cols[:, 1:]
    local = jnp.dot(link_float.T, solution_cols, precision=highest)
    total = butterfly_sum(local, ("tm", "scen", "line"))
    vec_total = total[:, 0]
    mat_total = total[:, 1:]
    inverse_count = 1.0 / (shards * lax.axis_size("scen") * lax.axis_size("line"))
    link_system = jnp.diag(link_diag) + inverse_count * mat_total
    right_side = inverse_count * vec_total - link_rhs
    link_lower = jnp.linalg.cholesky(link_system)
    link_step = jax.scipy.linalg.cho_solve((link_lower, True), right_side)
    newton_step = step_vec - jnp.dot(step_cols, link_step, precision=highest)
    return (newton_step[None, None], link_step)


def solution(mesh):
    return jax.shard_map(
        on_device,
        mesh=mesh,
        in_specs=(
            P("line", None, None),
            P(("scen", "line"), "tm", None),
            P(("scen", "line"), "tm", None, None),
            P(("scen", "line"), "tm", None),
            P(("scen", "line"), "tm", None),
            P(("scen", "line"), "tm", None, None),
            P(),
            P(),
            P(),
        ),
        out_specs=(P(("scen", "line"), "tm", None), P()),
        check_vma=False,
    )
```

profile of v0, /device:TPU:2, one launch (start us, length us, event | category | flops | bytes accessed | tf_op | source)
XLA Modules:
  0.0 658.7 jit_solution(9514112737942022669)
XLA Ops:
  12.1 141.1 %all-gather.2.cloned.1.call-done = bf16[64,128,1024]{2,1,0:T(8,128)(2,1)} async-done(((bf16[2,128,1024]{2,1,0:T(8,128)(2,1)}), bf16[64,128,1024]{2,1,0:T(8,128)(2,1)}) %all-gather.2.cloned.1.call-update) | async-done | bytes 16777232 | tf_op jit(solution)/shard_map/all_gather | solution.py:52
  153.3 6.4 gather_fusion
  170.7 11.7 %cholesky.243 = f32[128,128]{1,0:T(8,128)S(1)} custom-call(f32[128,128]{1,0:T(8,128)S(1)} %copy.59), custom_call_target="Cholesky" | custom-call | tf_op jit(solution)/shard_map/cholesky | solution.py:63
  182.5 9.8 %custom-call.59 = f32[1,128,128]{1,2,0:T(8,128)S(1)} custom-call(f32[1,128,128]{2,1,0:T(8,128)S(1)} %get-tuple-element.78), custom_call_target="InvertDiagBlocksLowerTriangular" | custom-call | tf_op jit(solution)/shard_map/cholesky | solution.py:63
  196.3 12.5 %cholesky.266 = f32[128,128]{1,0:T(8,128)S(1)} custom-call(f32[128,128]{1,0:T(8,128)} %copy.61), custom_call_target="Cholesky" | custom-call | tf_op jit(solution)/shard_map/cholesky | solution.py:63
  209.5 10.8 %custom-call.60 = f32[1,128,128]{1,2,0:T(8,128)S(1)} custom-call(f32[1,128,128]{2,1,0:T(8,128)} %get-tuple-element.75), custom_call_target="InvertDiagBlocksLowerTriangular" | custom-call | tf_op jit(solution)/shard_map/cholesky | solution.py:63
  223.3 12.5 %cholesky.293 = f32[128,128]{1,0:T(8,128)S(1)} custom-call(f32[128,128]{1,0:T(8,128)} %copy.63), custom_call_target="Cholesky" | custom-call | tf_op jit(solution)/shard_map/cholesky | solution.py:63
  236.6 9.8 %custom-call.67 = f32[1,128,128]{1,2,0:T(8,128)S(1)} custom-call(f32[1,128,128]{2,1,0:T(8,128)S(1)} %get-tuple-element.72), custom_call_target="InvertDiagBlocksLowerTriangular" | custom-call | tf_op jit(solution)/shard_map/cholesky/custom-call.17 | solution.py:63
  248.6 12.2 %cholesky.522 = f32[128,128]{1,0:T(8,128)S(1)} custom-call(f32[128,128]{1,0:T(8,128)S(1)} %copy.66), custom_call_target="Cholesky" | custom-call | tf_op jit(solution)/shard_map/cholesky | solution.py:63
  261.5 9.8 %custom-call.68 = f32[1,128,128]{1,2,0:T(8,128)S(1)} custom-call(f32[1,128,128]{2,1,0:T(8,128)S(1)} %get-tuple-element.69), custom_call_target="InvertDiagBlocksLowerTriangular" | custom-call | tf_op jit(solution)/shard_map/cholesky/custom-call.18 | solution.py:63
  273.4 11.7 %cholesky.537 = f32[128,128]{1,0:T(8,128)S(1)} custom-call(f32[128,128]{1,0:T(8,128)S(1)} %copy.69), custom_call_target="Cholesky" | custom-call | tf_op jit(solution)/shard_map/cholesky | solution.py:63
  285.8 9.8 %custom-call.69 = f32[1,128,128]{1,2,0:T(8,128)S(1)} custom-call(f32[1,128,128]{2,1,0:T(8,128)S(1)} %get-tuple-element.66), custom_call_target="InvertDiagBlocksLowerTriangular" | custom-call | tf_op jit(solution)/shard_map/cholesky/custom-call.19 | solution.py:63
  297.3 11.9 %cholesky.551 = f32[128,128]{1,0:T(8,128)S(1)} custom-call(f32[128,128]{1,0:T(8,128)S(1)} %copy.72), custom_call_target="Cholesky" | custom-call | tf_op jit(solution)/shard_map/cholesky | solution.py:63
  316.0 21.1 %while.2 = (s32[]{:T(128)}, f32[768,768]{1,0:T(8,128)}, s32[6,2]{0,1:T(2,128)S(1)}, f32[6,128,128]{2,1,0:T(8,128)}, s32[]{:T(128)}) while((s32[]{:T(128)}, f32[768,768]{1,0:T(8,128)}, s32[6,2]{0,1:T(2,128)S(1)}, f32[6,128,128]{2,1,0:T(8,128)}, s32[]{:T(128)}) %tuple.70), condition=%wide.while_cond, body=%wide.while_body.sunk | while | flops 2 | bytes 132705 | solution.py:34
  337.1 59.8 %custom-call.61 = f32[6,128,128]{1,2,0:T(8,128)S(1)} custom-call(f32[6,128,128]{2,1,0:T(8,128)} %get-tuple-element.12), custom_call_target="InvertDiagBlocksLowerTriangular" | custom-call | tf_op jit(solution)/shard_map/triangular_solve | solution.py:34
  418.7 11.7 %cholesky.565 = f32[128,128]{1,0:T(8,128)S(1)} custom-call(f32[128,128]{1,0:T(8,128)S(1)} %cholesky.649), custom_call_target="Cholesky" | custom-call | tf_op jit(solution)/shard_map/cholesky | solution.py:82
  430.6 9.8 %custom-call.70 = f32[1,128,128]{1,2,0:T(8,128)S(1)} custom-call(f32[1,128,128]{2,1,0:T(8,128)S(1)} %get-tuple-element.62), custom_call_target="InvertDiagBlocksLowerTriangular" | custom-call | tf_op jit(solution)/shard_map/cholesky/custom-call.17 | solution.py:82
  442.9 11.7 %cholesky.576 = f32[128,128]{1,0:T(8,128)S(1)} custom-call(f32[128,128]{1,0:T(8,128)S(1)} %cholesky.653), custom_call_target="Cholesky" | custom-call | tf_op jit(solution)/shard_map/cholesky | solution.py:82
  455.9 10.0 %custom-call.71 = f32[1,128,128]{1,2,0:T(8,128)S(1)} custom-call(f32[1,128,128]{2,1,0:T(8,128)S(1)} %get-tuple-element.59), custom_call_target="InvertDiagBlocksLowerTriangular" | custom-call | tf_op jit(solution)/shard_map/cholesky/custom-call.18 | solution.py:82
  467.5 11.7 %cholesky.593 = f32[128,128]{1,0:T(8,128)S(1)} custom-call(f32[128,128]{1,0:T(8,128)S(1)} %cholesky.658), custom_call_target="Cholesky" | custom-call | tf_op jit(solution)/shard_map/cholesky | solution.py:82
  479.8 9.8 %custom-call.72 = f32[1,128,128]{1,2,0:T(8,128)S(1)} custom-call(f32[1,128,128]{2,1,0:T(8,128)S(1)} %get-tuple-element.56), custom_call_target="InvertDiagBlocksLowerTriangular" | custom-call | tf_op jit(solution)/shard_map/cholesky/custom-call.19 | solution.py:82
  491.1 11.9 %cholesky.606 = f32[128,128]{1,0:T(8,128)S(1)} custom-call(f32[128,128]{1,0:T(8,128)S(1)} %convolution_subtract_fusion.23), custom_call_target="Cholesky" | custom-call | tf_op jit(solution)/shard_map/cholesky | solution.py:82
  506.4 10.9 %while.3 = (s32[]{:T(128)}, f32[512,512]{1,0:T(8,128)S(1)}, s32[4,2]{0,1:T(2,128)S(1)}, f32[4,128,128]{2,1,0:T(8,128)}, s32[]{:T(128)}) while((s32[]{:T(128)}, f32[512,512]{1,0:T(8,128)S(1)}, s32[4,2]{0,1:T(2,128)S(1)}, f32[4,128,128]{2,1,0:T(8,128)}, s32[]{:T(128)}) %tuple.73), condition=%wide.while_cond.1, body=%wide.while_body.1.sunk | while | flops 2 | bytes 132705 | solution.py:83
  517.3 40.1 %custom-call.62 = f32[4,128,128]{1,2,0:T(8,128)S(1)} custom-call(f32[4,128,128]{2,1,0:T(8,128)} %get-tuple-element.20), custom_call_target="InvertDiagBlocksLowerTriangular" | custom-call | tf_op jit(solution)/shard_map/jit(_cho_solve)/triangular_solve | solution.py:83
  576.7 5.0 collective-permute-done.2
  588.6 5.1 collective-permute-done.4
  595.2 5.4 collective-permute-done.5
  600.7 5.4 collective-permute-done.6
  608.1 8.2 %collective-permute-done.7 = f32[128,129]{1,0:T(8,128)S(1)} collective-permute-done((f32[128,129]{1,0:T(8,128)S(1)}, f32[128,129]{1,0:T(8,128)S(1)}, u32[]{:S(2)}, u32[]{:S(2)}) %collective-permute-start.7) | collective-permute-done | bytes 66080 | tf_op jit(solution)/shard_map/ppermute | solution.py:28
  620.1 6.6 %collective-permute-done.8 = f32[128,129]{1,0:T(8,128)S(1)} collective-permute-done((f32[128,129]{1,0:T(8,128)S(1)}, f32[128,129]{1,0:T(8,128)S(1)}, u32[]{:S(2)}, u32[]{:S(2)}) %collective-permute-start.8) | collective-permute-done | bytes 66080 | tf_op jit(solution)/shard_map/ppermute | solution.py:28
  627.2 11.7 %cholesky.617 = f32[128,128]{1,0:T(8,128)S(1)} custom-call(f32[128,128]{1,0:T(8,128)S(1)} %fusion.125), custom_call_target="Cholesky" | custom-call | tf_op jit(solution)/shard_map/jit(cholesky)/cholesky | solution.py:98
  640.2 9.8 %custom-call.63 = f32[1,128,128]{1,2,0:T(8,128)S(1)} custom-call(f32[1,128,128]{2,1,0:T(8,128)S(1)} %fusion.110), custom_call_target="InvertDiagBlocksLowerTriangular" | custom-call | tf_op jit(solution)/shard_map/jit(_cho_solve)/triangular_solve | solution.py:99
  (238 shorter events, 132.8 us)
Async XLA Ops:
  7.2 4.9 copy-start.21
  7.2 4.9 copy-start.15
  7.2 4.9 copy-start.16
  7.2 146.1 %all-gather.2.cloned.1.call-start = ((), (), s32[]{:S(2)}) async-start(), calls=%async_computation | async-start | bytes 17301504 | tf_op jit(solution)/shard_map/all_gather | solution.py:52
  9.8 0.8 copy-start.3
  10.6 149.1 %copy-start.20 = (f32[1,1,8,128]{3,2,1,0:T(8,128)S(1)}, f32[1,1,8,128]{3,2,1,0:T(8,128)}, u32[]{:S(2)}) copy-start(f32[1,1,8,128]{3,2,1,0:T(8,128)} %param.17) | copy-start | bytes 12292
  162.3 2.6 copy-start.1
  169.2 1.4 copy-start.2
  316.0 82.3 %copy-start = (f32[768,129]{0,1:T(8,128)S(1)}, f32[768,129]{0,1:T(8,128)}, u32[]{:S(2)}) copy-start(f32[768,129]{0,1:T(8,128)} %fusion.34) | copy-start | bytes 1188868
  396.9 11.7 %copy-start.11 = (f32[6,128,128]{1,2,0:T(8,128)}, f32[6,128,128]{1,2,0:T(8,128)S(1)}, u32[]{:S(2)}) copy-start(f32[6,128,128]{1,2,0:T(8,128)S(1)} %custom-call.61) | copy-start | bytes 1179652
  406.4 4.4 copy-start.4
  406.4 4.4 copy-start.14
  411.9 2.2 collective-permute-start
  412.4 2.7 copy-start.6
  414.1 0.8 copy-start.9
  414.2 0.9 copy-start.10
  414.2 1.0 copy-start.7
  415.2 0.7 copy-start.8
  417.7 1.0 copy-start.5
  561.5 4.3 copy-start.12
  567.2 6.9 %copy-start.13 = (bf16[1,1,1024,128]{3,2,1,0:T(8,128)(2,1)S(1)}, bf16[1,1,1024,128]{3,2,1,0:T(8,128)(2,1)}, u32[]{:S(2)}) copy-start(bf16[1,1,1024,128]{3,2,1,0:T(8,128)(2,1)} %param.20) | copy-start | bytes 786436
  574.0 52.8 %copy-start.17 = (f32[128]{0:T(128)S(1)}, f32[128]{0:T(128)}, u32[]{:S(2)}) copy-start(f32[128]{0:T(128)} %param.22) | copy-start | bytes 1540
  574.1 75.9 %copy-start.19 = (f32[128]{0:T(128)S(1)}, f32[128]{0:T(128)}, u32[]{:S(2)}) copy-start(f32[128]{0:T(128)} %param.23) | copy-start | bytes 1540
  574.6 1.4 collective-permute-start.1
  576.1 5.6 collective-permute-start.2
  581.7 6.6 collective-permute-start.3
  588.3 5.4 collective-permute-start.4
  593.8 6.8 %collective-permute-start.5 = (f32[128,129]{1,0:T(8,128)S(1)}, f32[128,129]{1,0:T(8,128)S(1)}, u32[]{:S(2)}, u32[]{:S(2)}) collective-permute-start(f32[128,129]{1,0:T(8,128)S(1)} %add.143), channel_id=1, source_target_pairs={{0,2},{1,3},{2,0},{3,1},{4,6},{5,7},{6,4},{7,5},{8,10},{9,11},{10,... | collective-permute-start | bytes 198152 | tf_op jit(solution)/shard_map/ppermute | solution.py:28
  600.6 5.5 collective-permute-start.6
  606.1 10.2 %collective-permute-start.7 = (f32[128,129]{1,0:T(8,128)S(1)}, f32[128,129]{1,0:T(8,128)S(1)}, u32[]{:S(2)}, u32[]{:S(2)}) collective-permute-start(f32[128,129]{1,0:T(8,128)S(1)} %add.145), channel_id=1, source_target_pairs={{0,8},{1,9},{2,10},{3,11},{4,12},{5,13},{6,14},{7,15},{8,0},{9,1},... | collective-permute-start | bytes 198152 | tf_op jit(solution)/shard_map/ppermute | solution.py:28
  616.3 10.4 %collective-permute-start.8 = (f32[128,129]{1,0:T(8,128)S(1)}, f32[128,129]{1,0:T(8,128)S(1)}, u32[]{:S(2)}, u32[]{:S(2)}) collective-permute-start(f32[128,129]{1,0:T(8,128)S(1)} %add.146), channel_id=1, source_target_pairs={{0,16},{1,17},{2,18},{3,19},{4,20},{5,21},{6,22},{7,23},{8,24},{9,... | collective-permute-start | bytes 198152 | tf_op jit(solution)/shard_map/ppermute | solution.py:28
  650.4 1.1 copy-start.18
Sparse Core Ops, SparseCore 0:
  10.6 142.6 all-gather.1
where the time goes:
time: 664 us; the launch traced here: 659 us
  other arithmetic  337 us (51%)
  waiting for transfers between devices  185 us (28%)
  local copies, waits for them, and re-layouts  51.9 us (8%)
  matrix products  51.5 us (8%)
  between operations  21.9 us (3%)
  starting transfers between devices  11.1 us (2%)
    all_gather x1, waiting for transfers between devices, on_device(): every_block = lax.all_gather(line_blocks, 'line', axis=0, tiled=True)  141 us
    another operation x22, other arithmetic, on_device(): l_nn = lax.linalg.cholesky(h_nn)  127 us
    another operation x15, other arithmetic, on_device(): lower = lax.linalg.cholesky(system)  79.4 us
    another operation x3, other arithmetic, trsm(): lax.linalg.triangular_solve(a, b, left_side=True, lower=True, transpose_a...  61.4 us
    ppermute x8, waiting for transfers between devices, butterfly_sum(): value = value + lax.ppermute(value, axis, pairs)  41.3 us
    another operation x3, other arithmetic, on_device(): jax.scipy.linalg.cho_solve((lower, True), jnp.concatenate([part0[:, count...  40.3 us
    another operation x30, local copies, waits for them, and re-layouts  32 us
    another operation x22, matrix products, trsm(): lax.linalg.triangular_solve(a, b, left_side=True, lower=True, transpose_a...  20.2 us
  transfers between devices with their start and end apart: 10, of which 10 were waited for; matrix products, arithmetic and copies ran while one was open for 1% of the time, Pallas kernels for 0%

commit v1 on v0

--- a/solution.py
+++ b/solution.py
@@ -45,11 +45,19 @@
     link_diag,
     link_rhs,
 ):
+
+    def direct_scales(matrix, dim_no):
+        piece_now = lax.axis_size("line")
+        a_now = jnp.stack(piece_now * [matrix])
+        base_arr = lax.all_to_all(a_now, "line", 0, 0)
+        d_next = jnp.concatenate(base_arr, axis=dim_no)
+        return d_next
+
     block_ids = binding[0, 0]
     order = line_blocks.shape[2]
     count = ramp_weight.shape[0]
     links = link_columns.shape[-1]
-    every_block = lax.all_gather(line_blocks, "line", axis=0, tiled=True)
+    every_block = direct_scales(line_blocks, 0)
     selected = jnp.take(every_block, block_ids, axis=0)
     shard = lax.axis_index("tm")
     shards = lax.axis_size("tm")

time: 664 us -> 929 us (1.40)
  waiting for transfers between devices: 185 us -> 420 us
  starting transfers between devices: 11.1 us -> 47 us
  between operations: 21.9 us -> 8.53 us
    all_to_all x0 -> x1, waiting for transfers between devices: none -> 379 us  [direct_scales(): base_arr = lax.all_to_all(a_now, 'line', 0, 0)]
    all_gather x1 -> x0, waiting for transfers between devices: 141 us -> none  [on_device(): every_block = lax.all_gather(line_blocks, 'line', axis=0, tiled=True)]
    ppermute x8, starting transfers between devices: 10.6 us -> 34.8 us  [butterfly_sum(): value = value + lax.ppermute(value, axis, pairs)]
    all_to_all x0 -> x1, starting transfers between devices: none -> 11.8 us  [direct_scales(): base_arr = lax.all_to_all(a_now, 'line', 0, 0)]
    another operation x30 -> x31, local copies, waits for them, and re-layouts: 32 us -> 38.8 us
  transfers between devices with their start and end apart: 10 -> 10, of which waited for: 10 -> 10; matrix products, arithmetic and copies ran while one was open for 1% -> 0% of each run, Pallas kernels for 0% -> 0%
where the time goes in v1:
time: 929 us; the launch traced here: 922 us
  waiting for transfers between devices  420 us (45%)
  other arithmetic  337 us (36%)
  local copies, waits for them, and re-layouts  58.1 us (6%)
  matrix products  51.6 us (6%)
  starting transfers between devices  47 us (5%)
    all_to_all x1, waiting for transfers between devices, direct_scales(): base_arr = lax.all_to_all(a_now, 'line', 0, 0)  379 us
    another operation x22, other arithmetic, on_device(): l_nn = lax.linalg.cholesky(h_nn)  127 us
    another operation x15, other arithmetic, on_device(): lower = lax.linalg.cholesky(system)  79.4 us
    another operation x3, other arithmetic, trsm(): lax.linalg.triangular_solve(a, b, left_side=True, lower=True, transpose_a...  61.9 us
    another operation x3, other arithmetic, on_device(): jax.scipy.linalg.cho_solve((lower, True), jnp.concatenate([part0[:, count...  40.3 us
    ppermute x8, waiting for transfers between devices, butterfly_sum(): value = value + lax.ppermute(value, axis, pairs)  39.3 us
    ppermute x8, starting transfers between devices, butterfly_sum(): value = value + lax.ppermute(value, axis, pairs)  34.8 us
    another operation x30, local copies, waits for them, and re-layouts  31.9 us
  transfers between devices with their start and end apart: 10, of which 10 were waited for; matrix products, arithmetic and copies ran while one was open for 0% of the time, Pallas kernels for 0%

profile of v1, /device:TPU:2, one launch (start us, length us, event | category | flops | bytes accessed | tf_op | source)
XLA Modules:
  0.0 922.3 jit_solution(1349521557896544419)
XLA Ops:
  0.6 6.8 stack.2
  7.5 11.8 %all-to-all-start = ((bf16[32,2,128,1024]{3,2,1,0:T(8,128)(2,1)}), bf16[32,2,128,1024]{3,2,1,0:T(8,128)(2,1)}, u32[]{:S(2)}, u32[]{:S(2)}) async-start(bf16[32,2,128,1024]{3,2,1,0:T(8,128)(2,1)} %stack.2), calls=%async_computation | async-start | bytes 33554432 | tf_op jit(solution)/shard_map/all_to_all | solution.py:52
  21.7 379.5 %all-to-all-done = bf16[32,2,128,1024]{3,2,1,0:T(8,128)(2,1)} async-done(((bf16[32,2,128,1024]{3,2,1,0:T(8,128)(2,1)}), bf16[32,2,128,1024]{3,2,1,0:T(8,128)(2,1)}, u32[]{:S(2)}, u32[]{:S(2)}) %all-to-all-start) | async-done | bytes 16777248 | tf_op jit(solution)/shard_map/all_to_all | solution.py:52
  401.2 6.4 gather_fusion
  419.0 11.7 %cholesky.243 = f32[128,128]{1,0:T(8,128)S(1)} custom-call(f32[128,128]{1,0:T(8,128)S(1)} %copy.36), custom_call_target="Cholesky" | custom-call | tf_op jit(solution)/shard_map/cholesky | solution.py:71
  430.8 9.8 %custom-call.59 = f32[1,128,128]{1,2,0:T(8,128)S(1)} custom-call(f32[1,128,128]{2,1,0:T(8,128)S(1)} %get-tuple-element.78), custom_call_target="InvertDiagBlocksLowerTriangular" | custom-call | tf_op jit(solution)/shard_map/cholesky | solution.py:71
  444.6 12.5 %cholesky.266 = f32[128,128]{1,0:T(8,128)S(1)} custom-call(f32[128,128]{1,0:T(8,128)} %copy.38), custom_call_target="Cholesky" | custom-call | tf_op jit(solution)/shard_map/cholesky | solution.py:71
  457.8 10.8 %custom-call.60 = f32[1,128,128]{1,2,0:T(8,128)S(1)} custom-call(f32[1,128,128]{2,1,0:T(8,128)} %get-tuple-element.75), custom_call_target="InvertDiagBlocksLowerTriangular" | custom-call | tf_op jit(solution)/shard_map/cholesky | solution.py:71
  471.5 12.5 %cholesky.293 = f32[128,128]{1,0:T(8,128)S(1)} custom-call(f32[128,128]{1,0:T(8,128)} %copy.40), custom_call_target="Cholesky" | custom-call | tf_op jit(solution)/shard_map/cholesky | solution.py:71
  484.8 9.8 %custom-call.67 = f32[1,128,128]{1,2,0:T(8,128)S(1)} custom-call(f32[1,128,128]{2,1,0:T(8,128)S(1)} %get-tuple-element.72), custom_call_target="InvertDiagBlocksLowerTriangular" | custom-call | tf_op jit(solution)/shard_map/cholesky/custom-call.17 | solution.py:71
  496.9 12.1 %cholesky.522 = f32[128,128]{1,0:T(8,128)S(1)} custom-call(f32[128,128]{1,0:T(8,128)S(1)} %copy.43), custom_call_target="Cholesky" | custom-call | tf_op jit(solution)/shard_map/cholesky | solution.py:71
  509.7 9.8 %custom-call.68 = f32[1,128,128]{1,2,0:T(8,128)S(1)} custom-call(f32[1,128,128]{2,1,0:T(8,128)S(1)} %get-tuple-element.69), custom_call_target="InvertDiagBlocksLowerTriangular" | custom-call | tf_op jit(solution)/shard_map/cholesky/custom-call.18 | solution.py:71
  521.6 11.7 %cholesky.537 = f32[128,128]{1,0:T(8,128)S(1)} custom-call(f32[128,128]{1,0:T(8,128)S(1)} %copy.46), custom_call_target="Cholesky" | custom-call | tf_op jit(solution)/shard_map/cholesky | solution.py:71
  534.0 9.8 %custom-call.69 = f32[1,128,128]{1,2,0:T(8,128)S(1)} custom-call(f32[1,128,128]{2,1,0:T(8,128)S(1)} %get-tuple-element.66), custom_call_target="InvertDiagBlocksLowerTriangular" | custom-call | tf_op jit(solution)/shard_map/cholesky/custom-call.19 | solution.py:71
  545.5 11.9 %cholesky.551 = f32[128,128]{1,0:T(8,128)S(1)} custom-call(f32[128,128]{1,0:T(8,128)S(1)} %copy.49), custom_call_target="Cholesky" | custom-call | tf_op jit(solution)/shard_map/cholesky | solution.py:71
  564.2 21.1 %while.2 = (s32[]{:T(128)}, f32[768,768]{1,0:T(8,128)}, s32[6,2]{0,1:T(2,128)S(1)}, f32[6,128,128]{2,1,0:T(8,128)}, s32[]{:T(128)}) while((s32[]{:T(128)}, f32[768,768]{1,0:T(8,128)}, s32[6,2]{0,1:T(2,128)S(1)}, f32[6,128,128]{2,1,0:T(8,128)}, s32[]{:T(128)}) %tuple.70), condition=%wide.while_cond, body=%wide.while_body.sunk | while | flops 2 | bytes 132705 | solution.py:34
  585.3 59.8 %custom-call.61 = f32[6,128,128]{1,2,0:T(8,128)S(1)} custom-call(f32[6,128,128]{2,1,0:T(8,128)} %get-tuple-element.12), custom_call_target="InvertDiagBlocksLowerTriangular" | custom-call | tf_op jit(solution)/shard_map/triangular_solve | solution.py:34
  666.8 11.7 %cholesky.565 = f32[128,128]{1,0:T(8,128)S(1)} custom-call(f32[128,128]{1,0:T(8,128)S(1)} %cholesky.649), custom_call_target="Cholesky" | custom-call | tf_op jit(solution)/shard_map/cholesky | solution.py:90
  678.7 9.8 %custom-call.70 = f32[1,128,128]{1,2,0:T(8,128)S(1)} custom-call(f32[1,128,128]{2,1,0:T(8,128)S(1)} %get-tuple-element.62), custom_call_target="InvertDiagBlocksLowerTriangular" | custom-call | tf_op jit(solution)/shard_map/cholesky/custom-call.17 | solution.py:90
  691.1 11.7 %cholesky.576 = f32[128,128]{1,0:T(8,128)S(1)} custom-call(f32[128,128]{1,0:T(8,128)S(1)} %cholesky.653), custom_call_target="Cholesky" | custom-call | tf_op jit(solution)/shard_map/cholesky | solution.py:90
  704.1 10.0 %custom-call.71 = f32[1,128,128]{1,2,0:T(8,128)S(1)} custom-call(f32[1,128,128]{2,1,0:T(8,128)S(1)} %get-tuple-element.59), custom_call_target="InvertDiagBlocksLowerTriangular" | custom-call | tf_op jit(solution)/shard_map/cholesky/custom-call.18 | solution.py:90
  715.6 11.7 %cholesky.593 = f32[128,128]{1,0:T(8,128)S(1)} custom-call(f32[128,128]{1,0:T(8,128)S(1)} %cholesky.658), custom_call_target="Cholesky" | custom-call | tf_op jit(solution)/shard_map/cholesky | solution.py:90
  728.0 9.8 %custom-call.72 = f32[1,128,128]{1,2,0:T(8,128)S(1)} custom-call(f32[1,128,128]{2,1,0:T(8,128)S(1)} %get-tuple-element.56), custom_call_target="InvertDiagBlocksLowerTriangular" | custom-call | tf_op jit(solution)/shard_map/cholesky/custom-call.19 | solution.py:90
  739.2 11.9 %cholesky.606 = f32[128,128]{1,0:T(8,128)S(1)} custom-call(f32[128,128]{1,0:T(8,128)S(1)} %convolution_subtract_fusion.23), custom_call_target="Cholesky" | custom-call | tf_op jit(solution)/shard_map/cholesky | solution.py:90
  754.5 10.9 %while.3 = (s32[]{:T(128)}, f32[512,512]{1,0:T(8,128)S(1)}, s32[4,2]{0,1:T(2,128)S(1)}, f32[4,128,128]{2,1,0:T(8,128)}, s32[]{:T(128)}) while((s32[]{:T(128)}, f32[512,512]{1,0:T(8,128)S(1)}, s32[4,2]{0,1:T(2,128)S(1)}, f32[4,128,128]{2,1,0:T(8,128)}, s32[]{:T(128)}) %tuple.73), condition=%wide.while_cond.1, body=%wide.while_body.1.sunk | while | flops 2 | bytes 132705 | solution.py:91
  765.4 40.1 %custom-call.62 = f32[4,128,128]{1,2,0:T(8,128)S(1)} custom-call(f32[4,128,128]{2,1,0:T(8,128)} %get-tuple-element.20), custom_call_target="InvertDiagBlocksLowerTriangular" | custom-call | tf_op jit(solution)/shard_map/jit(_cho_solve)/triangular_solve | solution.py:91
  843.1 27.9 %collective-permute-start.5 = (f32[128,129]{1,0:T(8,128)S(1)}, f32[128,129]{1,0:T(8,128)S(1)}, u32[]{:S(2)}, u32[]{:S(2)}) collective-permute-start(f32[128,129]{1,0:T(8,128)S(1)} %add.143), channel_id=1, source_target_pairs={{0,2},{1,3},{2,0},{3,1},{4,6},{5,7},{6,4},{7,5},{8,10},{9,11},{10,... | collective-permute-start | bytes 198152 | tf_op jit(solution)/shard_map/ppermute | solution.py:28
  874.1 6.3 collective-permute-done.6
  880.5 7.6 collective-permute-done.7
  888.3 8.8 collective-permute-done.8
  897.6 11.7 %cholesky.617 = f32[128,128]{1,0:T(8,128)S(1)} custom-call(f32[128,128]{1,0:T(8,128)S(1)} %fusion.125), custom_call_target="Cholesky" | custom-call | tf_op jit(solution)/shard_map/jit(cholesky)/cholesky | solution.py:106
  910.6 9.8 %custom-call.63 = f32[1,128,128]{1,2,0:T(8,128)S(1)} custom-call(f32[1,128,128]{2,1,0:T(8,128)S(1)} %fusion.110), custom_call_target="InvertDiagBlocksLowerTriangular" | custom-call | tf_op jit(solution)/shard_map/jit(_cho_solve)/triangular_solve | solution.py:107
  (242 shorter events, 138.1 us)
Async XLA Ops:
  7.4 11.8 %copy-start.13 = (bf16[1,1,1024,128]{3,2,1,0:T(8,128)(2,1)S(1)}, bf16[1,1,1024,128]{3,2,1,0:T(8,128)(2,1)}, u32[]{:S(2)}) copy-start(bf16[1,1,1024,128]{3,2,1,0:T(8,128)(2,1)} %param.20) | copy-start | bytes 786436
  7.4 12.6 %copy-start.22 = (s32[1,1,8]{2,1,0:T(1,128)S(1)}, s32[1,1,8]{2,1,0:T(1,128)}, u32[]{:S(2)}) copy-start(s32[1,1,8]{2,1,0:T(1,128)} %param.16) | copy-start | bytes 100
  7.4 13.4 %copy-start.15 = (f32[1,1,1024]{2,1,0:T(1,128)S(1)}, f32[1,1,1024]{2,1,0:T(1,128)}, u32[]{:S(2)}) copy-start(f32[1,1,1024]{2,1,0:T(1,128)} %param.19) | copy-start | bytes 12292
  7.4 14.2 %copy-start.16 = (f32[256]{0:T(256)S(1)}, f32[256]{0:T(256)}, u32[]{:S(2)}) copy-start(f32[256]{0:T(256)} %param.21) | copy-start | bytes 3076
  7.5 14.2 %copy-start.17 = (f32[1,1,1024]{2,1,0:T(1,128)S(1)}, f32[1,1,1024]{2,1,0:T(1,128)}, u32[]{:S(2)}) copy-start(f32[1,1,1024]{2,1,0:T(1,128)} %param.18) | copy-start | bytes 12292
  7.5 393.7 %all-to-all-start = ((bf16[32,2,128,1024]{3,2,1,0:T(8,128)(2,1)}), bf16[32,2,128,1024]{3,2,1,0:T(8,128)(2,1)}, u32[]{:S(2)}, u32[]{:S(2)}) async-start(bf16[32,2,128,1024]{3,2,1,0:T(8,128)(2,1)} %stack.2), calls=%async_computation | async-start | bytes 33554432 | tf_op jit(solution)/shard_map/all_to_all | solution.py:52
  20.1 0.8 copy-start.3
  20.9 386.8 %copy-start.21 = (f32[1,1,8,128]{3,2,1,0:T(8,128)S(1)}, f32[1,1,8,128]{3,2,1,0:T(8,128)}, u32[]{:S(2)}) copy-start(f32[1,1,8,128]{3,2,1,0:T(8,128)} %param.17) | copy-start | bytes 12292
  410.3 2.6 copy-start.1
  417.5 1.4 copy-start.2
  562.5 1.6 copy-start.23
  564.2 82.3 %copy-start = (f32[768,129]{0,1:T(8,128)S(1)}, f32[768,129]{0,1:T(8,128)}, u32[]{:S(2)}) copy-start(f32[768,129]{0,1:T(8,128)} %fusion.34) | copy-start | bytes 1188868
  645.0 11.7 %copy-start.11 = (f32[6,128,128]{1,2,0:T(8,128)}, f32[6,128,128]{1,2,0:T(8,128)S(1)}, u32[]{:S(2)}) copy-start(f32[6,128,128]{1,2,0:T(8,128)S(1)} %custom-call.61) | copy-start | bytes 1179652
  654.6 4.4 copy-start.4
  660.0 2.2 collective-permute-start
  660.6 2.7 copy-start.6
  662.3 0.9 copy-start.10
  662.3 1.0 copy-start.7
  665.8 1.0 copy-start.5
  809.6 4.5 copy-start.12
  815.5 6.9 copy-start.14
  822.3 74.9 %copy-start.18 = (f32[128]{0:T(128)S(1)}, f32[128]{0:T(128)}, u32[]{:S(2)}) copy-start(f32[128]{0:T(128)} %param.22) | copy-start | bytes 1540
  822.4 98.0 %copy-start.20 = (f32[128]{0:T(128)S(1)}, f32[128]{0:T(128)}, u32[]{:S(2)}) copy-start(f32[128]{0:T(128)} %param.23) | copy-start | bytes 1540
  822.9 1.4 collective-permute-start.1
  824.4 5.6 collective-permute-start.2
  830.0 6.6 collective-permute-start.3
  836.6 6.5 collective-permute-start.4
  843.1 30.8 %collective-permute-start.5 = (f32[128,129]{1,0:T(8,128)S(1)}, f32[128,129]{1,0:T(8,128)S(1)}, u32[]{:S(2)}, u32[]{:S(2)}) collective-permute-start(f32[128,129]{1,0:T(8,128)S(1)} %add.143), channel_id=1, source_target_pairs={{0,2},{1,3},{2,0},{3,1},{4,6},{5,7},{6,4},{7,5},{8,10},{9,11},{10,... | collective-permute-start | bytes 198152 | tf_op jit(solution)/shard_map/ppermute | solution.py:28
  874.0 6.4 collective-permute-start.6
  880.4 7.7 collective-permute-start.7
  888.2 9.0 collective-permute-start.8
  920.8 1.1 copy-start.19
  (2 other events, 1.5 us)
